TPU v7x, 32 devices: a whole 2x2x4 slice. The times are simulated.
32 devices in a mesh: tok: 8 (over z, x), grp: 4 (over y, core).
Axes of the slice: x: 2, y: 2, z: 4, core: 2. Of those that a mesh axis runs over, the one named last changes fastest.
Arguments:
- queries: bfloat16 [1536, 2048], P('tok', 'grp'), may hold values from -72 to 72
- new_keys: bfloat16 [1536, 2048], P('tok', 'grp'), may hold values from -8 to 8
- new_values: bfloat16 [1536, 2048], P('tok', 'grp'), may hold values from -6 to 6
- residual: bfloat16 [1536, 2048], P('tok', 'grp'), may hold values from -6 to 6
- w_out: bfloat16 [2048, 2048], P('grp'), may hold values from -0.125 to 0.125
- leaf_keys: bfloat16 [8, 512, 2048], P('tok', None, 'grp'), may hold values from -6 to 6
- leaf_values: bfloat16 [8, 512, 2048], P('tok', None, 'grp'), may hold values from -6 to 6
- upper_keys: bfloat16 [6, 1024, 2048], P(None, 'tok', 'grp'), may hold values from -8 to 8
- upper_values: bfloat16 [6, 1024, 2048], P(None, 'tok', 'grp'), may hold values from -6 to 6
- req_len: int32 [8], replicated, may hold values from 48 to 192, as said below
- leaf_mid: int32 [8], replicated, may hold values from 0 to 3
- mid_root: int32 [4], replicated, may hold values from 0 to 1, as said below
- upper_len: int32 [6], replicated, may hold values from 256 to 1024, as said below
- leaf_len: int32 [8], replicated, may hold values from 128 to 512, as said below
Outputs:
- hidden_out: bfloat16 [1536, 2048], P('tok', 'grp')
Inputs may be any that keep to these rules, and one draw needn't show every extreme that they name: `req_len`: some request has exactly 192 new tokens. `mid_root`: each root is the parent of 2 mids. `upper_len`: the first 2 entries are roots and equal 1024. `leaf_len`: some leaf has exactly 512 positions.
All inputs are finite; a program needn't handle non-finite values.
Results may differ from a plain program's by a relative error of at most 0.008.
Values may be sent and summed in bfloat16 or wider, within the bound.
No kernel may reach another device: no remote copies, remote signals or barrier semaphores. Data moves between devices by JAX's collectives and lax.ppermute only.
A program may use at most 64 MiB of HBM per device.

v0:
```python
import math
import jax
import jax.numpy as jnp
from jax import lax
from jax.sharding import PartitionSpec as P

HEAD_DIM = 128
NEG_FILL = -1e30


def partial_attention(query_rows, key_rows, values, allowed, head_count):
    head_width = query_rows.shape[1] // head_count
    query_heads = query_rows.reshape(query_rows.shape[0], head_count, head_width)
    key_heads = key_rows.reshape(key_rows.shape[0], head_count, head_width)
    value_heads = values.reshape(values.shape[0], head_count, head_width)
    scores = jnp.einsum(
        "qhd,khd->hqk", query_heads, key_heads, preferred_element_type=jnp.float32
    ) * head_width ** (-0.5)
    scores = jnp.where(allowed[None], scores, NEG_FILL)
    row_max = jnp.max(scores, axis=2)
    exp_scores = jnp.where(allowed[None], jnp.exp(scores - row_max[:, :, None]), 0.0)
    row_total = jnp.sum(exp_scores, axis=2)
    weighted = jnp.einsum(
        "hqk,khd->hqd",
        exp_scores.astype(jnp.bfloat16),
        value_heads,
        preferred_element_type=jnp.float32,
    )
    return (row_max, row_total, weighted)


def combine(earlier, latter):
    new_max = jnp.maximum(earlier[0], latter[0])
    earlier_scale = jnp.exp(earlier[0] - new_max)
    latter_scale = jnp.exp(latter[0] - new_max)
    return (
        new_max,
        earlier[1] * earlier_scale + latter[1] * latter_scale,
        earlier[2] * earlier_scale[:, :, None] + latter[2] * latter_scale[:, :, None],
    )


def node_attention(carry, query_rows, node_keys, node_values, node_len, head_count):
    node_rows = node_keys.shape[0]
    block = math.gcd(node_rows, 512)
    row_count = query_rows.shape[0]
    for start in range(0, node_rows, block):
        positions = start + jnp.arange(block, dtype=jnp.int32)
        allowed = jnp.broadcast_to((positions < node_len)[None, :], (row_count, block))
        piece_part = partial_attention(
            query_rows,
            node_keys[start : start + block],
            node_values[start : start + block],
            allowed,
            head_count,
        )
        carry = combine(carry, piece_part)
    return carry


def shards(
    queries,
    new_keys,
    new_values,
    residual,
    w_out,
    leaf_keys,
    leaf_values,
    upper_keys,
    upper_values,
    req_len,
    leaf_mid,
    mid_root,
    upper_len,
    leaf_len,
):
    dev_count = lax.axis_size("tok")
    my_index = lax.axis_index("tok")
    row_count = queries.shape[0]
    col_count = queries.shape[1]
    head_count = col_count // HEAD_DIM
    mid_count = mid_root.shape[0]
    node_count = upper_len.shape[0]
    root_count = node_count - mid_count
    owned = (jnp.arange(dev_count, dtype=jnp.int32) == my_index).astype(jnp.int32)
    my_length = jnp.sum(owned * req_len)
    my_mid = jnp.sum(owned * leaf_mid)
    my_leaf_len = jnp.sum(owned * leaf_len)
    my_root = jnp.sum((jnp.arange(mid_count) == my_mid).astype(jnp.int32) * mid_root)
    node_ids = jnp.arange(node_count)
    root_len = jnp.sum((node_ids == my_root).astype(jnp.int32) * upper_len)
    mid_len = jnp.sum((node_ids == root_count + my_mid).astype(jnp.int32) * upper_len)
    position = jnp.arange(row_count, dtype=jnp.int32)
    is_live = position < my_length
    leaf_count = leaf_keys.shape[1]
    local_keys = jnp.concatenate([leaf_keys[0], new_keys], axis=0)
    local_values = jnp.concatenate([leaf_values[0], new_values], axis=0)
    leaf_allowed = jnp.broadcast_to(
        (jnp.arange(leaf_count) < my_leaf_len)[None, :], (row_count, leaf_count)
    )
    new_allowed = (position[None, :] <= position[:, None]) & is_live[None, :]
    local_part = partial_attention(
        queries,
        local_keys,
        local_values,
        jnp.concatenate([leaf_allowed, new_allowed], axis=1),
        head_count,
    )
    gathered_keys, gathered_values = (
        lax.all_gather(upper_keys, "tok", axis=1, tiled=True),
        lax.all_gather(upper_values, "tok", axis=1, tiled=True),
    )
    merged = node_attention(
        local_part, queries, gathered_keys[my_root], gathered_values[my_root], root_len, head_count
    )
    merged = node_attention(
        merged,
        queries,
        gathered_keys[root_count + my_mid],
        gathered_values[root_count + my_mid],
        mid_len,
        head_count,
    )
    attended = (merged[2] / merged[1][:, :, None]).transpose(1, 0, 2).reshape(row_count, col_count)
    attention = jnp.where(is_live[:, None], attended, 0.0).astype(jnp.bfloat16)
    projected = jnp.dot(attention, w_out, preferred_element_type=jnp.float32)
    mixed = lax.psum_scatter(
        projected.astype(jnp.bfloat16), "grp", scatter_dimension=1, tiled=True
    ).astype(jnp.float32)
    return (residual.astype(jnp.float32) + mixed).astype(jnp.bfloat16)


def solution(mesh):
    in_specs = (
        P("tok", "grp"),
        P("tok", "grp"),
        P("tok", "grp"),
        P("tok", "grp"),
        P("grp", None),
        P("tok", None, "grp"),
        P("tok", None, "grp"),
        P(None, "tok", "grp"),
        P(None, "tok", "grp"),
        P(),
        P(),
        P(),
        P(),
        P(),
    )
    out_specs = P("tok", "grp")
    return jax.shard_map(shards, mesh=mesh, in_specs=in_specs, out_specs=out_specs, check_vma=False)
```

profile of v0, /device:TPU:0, one launch (start us, length us, event | category | flops | bytes accessed | tf_op | source)
XLA Modules:
  0.0 251.3 jit_solution(10677370438847150841)
XLA Ops:
  6.5 2.5 copy.27
  9.1 1.2 copy.30
  10.4 0.6 select_reduce_fusion
  12.3 1.3 fusion.91
  15.1 1.0 copy.21
  16.2 1.3 copy.24
  18.3 0.6 iota_compare_fusion.3
  18.9 1.2 fusion.92
  20.2 0.6 iota_compare_fusion.1
  20.8 0.6 fusion.89
  21.4 0.7 fusion.90
  22.0 0.7 iota_compare_fusion.2
  22.7 0.6 select_reduce_fusion.2
  23.3 0.6 iota_compare_fusion.4
  24.1 1.0 copy_bitcast_fusion
  25.1 1.7 fusion
  26.9 1.4 copy-done.10
  28.3 0.9 fusion.1
  29.1 82.9 %all-gather.3.cloned.1.call-done = bf16[6,1024,512]{1,2,0:T(8,128)(2,1)} async-done(((bf16[6,128,512]{1,2,0:T(8,128)(2,1)}), bf16[6,1024,512]{1,2,0:T(8,128)(2,1)}) %all-gather.3.cloned.1.call-update) | async-done | bytes 6291472 | tf_op jit(solution)/shard_map/all_gather | solution.py:110
  112.1 1.7 constant_dynamic-slice_fusion.3
  114.2 0.5 fusion.17
  117.7 1.1 copy-done.7
  119.4 92.8 %all-gather.5.cloned.1.call-done = bf16[6,1024,512]{1,2,0:T(8,128)(2,1)} async-done(((bf16[6,128,512]{1,2,0:T(8,128)(2,1)}), bf16[6,1024,512]{1,2,0:T(8,128)(2,1)}) %all-gather.5.cloned.1.call-update) | async-done | bytes 6291472 | tf_op jit(solution)/shard_map/all_gather | solution.py:111
  212.3 1.8 constant_dynamic-slice_fusion.4
  214.8 0.7 copy-done.8
  216.0 0.6 copy-done.11
  216.6 1.0 fusion.31
  218.0 0.6 fusion.32
  218.5 0.8 copy-done.4
  219.9 1.5 convolution_convert_fusion
  221.4 21.6 %reduce-scatter.2.cloned.1.call-done = bf16[192,512]{1,0:T(8,128)(2,1)} async-done(((bf16[192,2048]{1,0:T(8,128)(2,1)}), bf16[192,512]{1,0:T(8,128)(2,1)}) %reduce-scatter.2.cloned.1.call-update) | async-done | bytes 196624 | tf_op jit(solution)/shard_map/reduce_scatter | solution.py:127
  243.1 1.7 add_convert_fusion
  (60 shorter events, 6.9 us)
Async XLA Ops:
  6.5 213.3 %copy-start = (bf16[512,2048]{1,0:T(8,128)(2,1)S(1)}, bf16[512,2048]{1,0:T(8,128)(2,1)}, u32[]{:S(2)}) copy-start(bf16[512,2048]{1,0:T(8,128)(2,1)} %param.18) | copy-start | bytes 6291460
  6.5 2.6 %copy-start.12 = (bf16[6,128,512]{2,1,0:T(8,128)(2,1)S(1)}, bf16[6,128,512]{2,1,0:T(8,128)(2,1)}, u32[]{:S(2)}) copy-start(bf16[6,128,512]{2,1,0:T(8,128)(2,1)} %param.22) | copy-start | bytes 2359300
  6.5 105.5 %all-gather.3.cloned.1.call-start = ((), (), s32[]{:S(2)}) async-start(), calls=%async_computation.1 | async-start | bytes 7077888 | tf_op jit(solution)/shard_map/all_gather | solution.py:110
  9.0 1.3 copy-start.16
  9.0 1.4 copy-start.17
  9.0 3.3 %copy-start.19 = (s32[4]{0:T(128)S(1)}, s32[4]{0:T(128)}, u32[]{:S(2)}) copy-start(s32[4]{0:T(128)} %param.25) | copy-start | bytes 52
  9.0 5.8 %copy-start.13 = (bf16[1,512,512]{2,1,0:T(8,128)(2,1)S(1)}, bf16[1,512,512]{2,1,0:T(8,128)(2,1)}, u32[]{:S(2)}) copy-start(bf16[1,512,512]{2,1,0:T(8,128)(2,1)} %param.19) | copy-start | bytes 1572868
  9.0 203.2 %all-gather.5.cloned.1.call-start = ((), (), s32[]{:S(2)}) async-start(), calls=%async_computation.2 | async-start | bytes 7077888 | tf_op jit(solution)/shard_map/all_gather | solution.py:111
  10.3 232.8 %reduce-scatter.2.cloned.1.call-start = ((), (), s32[]{:S(2)}) async-start(), calls=%async_computation.3 | async-start | bytes 983040 | tf_op jit(solution)/shard_map/reduce_scatter | solution.py:127
  15.1 3.9 %copy-start.18 = (s32[6]{0:T(128)S(1)}, s32[6]{0:T(128)}, u32[]{:S(2)}) copy-start(s32[6]{0:T(128)} %param.26) | copy-start | bytes 76
  15.1 7.6 %copy-start.20 = (s32[8]{0:T(128)S(1)}, s32[8]{0:T(128)}, u32[]{:S(2)}) copy-start(s32[8]{0:T(128)} %param.23) | copy-start | bytes 100
  15.1 9.0 %copy-start.14 = (bf16[192,512]{1,0:T(8,128)(2,1)S(1)}, bf16[192,512]{1,0:T(8,128)(2,1)}, u32[]{:S(2)}) copy-start(bf16[192,512]{1,0:T(8,128)(2,1)} %param.15) | copy-start | bytes 589828
  16.2 8.9 %copy-start.9 = (bf16[192,512]{1,0:T(8,128)(2,1)S(1)}, bf16[192,512]{1,0:T(8,128)(2,1)}, u32[]{:S(2)}) copy-start(bf16[192,512]{1,0:T(8,128)(2,1)} %param.14) | copy-start | bytes 589828
  26.8 1.4 copy-start.10
  114.2 1.2 copy-start.3
  115.3 1.2 copy-start.5
  116.5 1.2 copy-start.1
  117.7 1.1 copy-start.7
  212.3 2.0 copy-start.6
  214.0 1.5 copy-start.8
  214.8 1.8 copy-start.11
  216.6 1.4 copy-start.2
  218.0 1.4 copy-start.4
  219.9 23.2 %copy-start.15 = (bf16[192,512]{1,0:T(8,128)(2,1)S(1)}, bf16[192,512]{1,0:T(8,128)(2,1)}, u32[]{:S(2)}) copy-start(bf16[192,512]{1,0:T(8,128)(2,1)} %param.17) | copy-start | bytes 589828
Sparse Core Ops, SparseCore 0:
  9.4 102.6 all-gather.2
  114.1 98.1 all-gather.4
  221.6 21.4 reduce-scatter.1
where the time goes:
time: 252 us; the launch traced here: 251 us
  waiting for transfers between devices  197 us (78%)
  local copies, waits for them, and re-layouts  16.9 us (7%)
  between operations  16.5 us (7%)
  other arithmetic  12.3 us (5%)
  matrix products  8.03 us (3%)
    all_gather x1, waiting for transfers between devices, shards(): lax.all_gather(upper_values, 'tok', axis=1, tiled=True)  92.8 us
    all_gather x1, waiting for transfers between devices, shards(): lax.all_gather(upper_keys, 'tok', axis=1, tiled=True)  82.9 us
    reduce_scatter x1, waiting for transfers between devices, shards(): lax.psum_scatter(projected.astype(jnp.bfloat16), 'grp', scatter_dimension...  21.6 us
    unnamed x46, local copies, waits for them, and re-layouts  11.2 us
  transfers between devices with their start and end apart: 3, of which 3 were waited for; matrix products, arithmetic and copies ran while one was open for 8% of the time, Pallas kernels for 0%

commit v1 on v0

--- a/solution.py
+++ b/solution.py
@@ -6,6 +6,27 @@
 
 HEAD_DIM = 128
 NEG_FILL = -1e30
+
+
+def collect(value, axis, dim):
+    size, here, extent = (lax.axis_size(axis), lax.axis_index(axis), value.shape[dim])
+    ahead = [(i, (i + 1) % size) for i in range(size)]
+    behind = [(i, (i - 1) % size) for i in range(size)]
+    result = jnp.zeros((*value.shape[:dim], size * extent, *value.shape[dim + 1 :]), value.dtype)
+    result = lax.dynamic_update_slice_in_dim(result, value, here * extent, axis=dim)
+    from_left = from_right = value
+    half = size // 2
+    for turn in range(1, half + 1):
+        from_left = lax.ppermute(from_left, axis, ahead)
+        result = lax.dynamic_update_slice_in_dim(
+            result, from_left, (here - turn) % size * extent, axis=dim
+        )
+        if turn < size - half:
+            from_right = lax.ppermute(from_right, axis, behind)
+            result = lax.dynamic_update_slice_in_dim(
+                result, from_right, (here + turn) % size * extent, axis=dim
+            )
+    return result
 
 
 def partial_attention(query_rows, key_rows, values, allowed, head_count):
@@ -107,7 +128,7 @@
         head_count,
     )
     gathered_keys, gathered_values = (
-        lax.all_gather(upper_keys, "tok", axis=1, tiled=True),
+        collect(upper_keys, "tok", 1),
         lax.all_gather(upper_values, "tok", axis=1, tiled=True),
     )
     merged = node_attention(

time: 252 us -> 240 us (0.952)
  waiting for transfers between devices: 197 us -> 158 us
  starting transfers between devices: 0.09 us -> 19.8 us
  local copies, waits for them, and re-layouts: 16.9 us -> 23.5 us
    ppermute x0 -> x7, waiting for transfers between devices: none -> 118 us  [the longest x4 105 us: collect(): from_left = lax.ppermute(from_left, axis, ahead)]
    all_gather x1 -> x0, waiting for transfers between devices: 82.9 us -> none  [shards(): lax.all_gather(upper_keys, 'tok', axis=1, tiled=True)]
    all_gather x1, waiting for transfers between devices: 92.8 us -> 17.3 us  [shards(): lax.all_gather(upper_values, 'tok', axis=1, tiled=True)]
    ppermute x0 -> x7, starting transfers between devices: none -> 19.7 us  [the longest x4 10.4 us: collect(): from_left = lax.ppermute(from_left, axis, ahead)]
    dynamic_update_slice x0 -> x8, local copies, waits for them, and re-layouts: none -> 4.44 us  [the longest x4 2.21 us: collect(): lax.dynamic_update_slice_in_dim(result, from_left, (here - turn) % size *...]
    unnamed x46 -> x44, local copies, waits for them, and re-layouts: 11.2 us -> 12.2 us
  transfers between devices with their start and end apart: 3 -> 9, of which waited for: 3 -> 8; matrix products, arithmetic and copies ran while one was open for 8% -> 12% of each run, Pallas kernels for 0% -> 0%
where the time goes in v1:
time: 240 us; the launch traced here: 239 us
  waiting for transfers between devices  158 us (66%)
  local copies, waits for them, and re-layouts  23.5 us (10%)
  starting transfers between devices  19.8 us (8%)
  between operations  17.2 us (7%)
  other arithmetic  12.6 us (5%)
  matrix products  8.03 us (3%)
    ppermute x4, waiting for transfers between devices, collect(): from_left = lax.ppermute(from_left, axis, ahead)  105 us
    reduce_scatter x1, waiting for transfers between devices, shards(): lax.psum_scatter(projected.astype(jnp.bfloat16), 'grp', scatter_dimension...  22.2 us
    all_gather x1, waiting for transfers between devices, shards(): lax.all_gather(upper_values, 'tok', axis=1, tiled=True)  17.3 us
    ppermute x3, waiting for transfers between devices, collect(): from_right = lax.ppermute(from_right, axis, behind)  13.8 us
    unnamed x44, local copies, waits for them, and re-layouts  12.2 us
    ppermute x4, starting transfers between devices, collect(): from_left = lax.ppermute(from_left, axis, ahead)  10.4 us
    ppermute x3, starting transfers between devices, collect(): from_right = lax.ppermute(from_right, axis, behind)  9.28 us
  transfers between devices with their start and end apart: 9, of which 8 were waited for; matrix products, arithmetic and copies ran while one was open for 12% of the time, Pallas kernels for 0%

profile of v1, /device:TPU:0, one launch (start us, length us, event | category | flops | bytes accessed | tf_op | source)
XLA Modules:
  0.0 239.0 jit_solution(7620667656248120337)
XLA Ops:
  6.5 2.4 %copy.32 = bf16[6,128,512]{1,2,0:T(8,128)(2,1)} copy(bf16[6,128,512]{2,1,0:T(8,128)(2,1)} %param.22) | data formatting | bytes 1572864 | tf_op args[8]
  9.1 1.5 copy.27
  10.6 3.0 %collective-permute-start = (bf16[6,128,512]{1,2,0:T(8,128)(2,1)S(1)}, bf16[6,128,512]{1,2,0:T(8,128)(2,1)}, u32[]{:S(2)}, u32[]{:S(2)}) collective-permute-start(bf16[6,128,512]{1,2,0:T(8,128)(2,1)S(1)} %copy.27), channel_id=1, source_target_pairs={{0,4},{4,8},{8,12},{12,16},{16,20},{20,24},{24,28},{28,0},{1,5},{5... | collective-permute-start | bytes 2359304 | tf_op jit(solution)/shard_map/ppermute | solution.py:20
  13.6 3.1 %collective-permute-start.1 = (bf16[6,128,512]{1,2,0:T(8,128)(2,1)S(1)}, bf16[6,128,512]{1,2,0:T(8,128)(2,1)}, u32[]{:S(2)}, u32[]{:S(2)}) collective-permute-start(bf16[6,128,512]{1,2,0:T(8,128)(2,1)S(1)} %copy.27), channel_id=1, source_target_pairs={{0,28},{4,0},{8,4},{12,8},{16,12},{20,16},{24,20},{28,24},{1,29},{... | collective-permute-start | bytes 2359304 | tf_op jit(solution)/shard_map/ppermute | solution.py:25
  18.7 1.4 fusion.91
  21.5 1.3 copy.20
  22.8 1.0 copy.21
  23.8 2.1 copy.24
  25.9 2.0 copy.25
  29.3 1.4 fusion.92
  33.3 22.3 %collective-permute-done = bf16[6,128,512]{1,2,0:T(8,128)(2,1)} collective-permute-done((bf16[6,128,512]{1,2,0:T(8,128)(2,1)S(1)}, bf16[6,128,512]{1,2,0:T(8,128)(2,1)}, u32[]{:S(2)}, u32[]{:S(2)}) %collective-permute-start) | collective-permute-done | bytes 786464 | tf_op jit(solution)/shard_map/ppermute | solution.py:20
  55.7 2.6 %collective-permute-start.2 = (bf16[6,128,512]{1,2,0:T(8,128)(2,1)}, bf16[6,128,512]{1,2,0:T(8,128)(2,1)S(1)}, u32[]{:S(2)}, u32[]{:S(2)}) collective-permute-start(bf16[6,128,512]{1,2,0:T(8,128)(2,1)} %collective-permute-done), channel_id=1, source_target_pairs={{0,4},{4,8},{8,12},{12,16},{16,20},{20,24},{24,28},{28,0},{1,5},{5... | collective-permute-start | bytes 2359304 | tf_op jit(solution)/shard_map/ppermute | solution.py:20
  58.3 1.0 copy_bitcast_fusion
  59.3 3.1 %collective-permute-start.3 = (bf16[6,128,512]{1,2,0:T(8,128)(2,1)}, bf16[6,128,512]{1,2,0:T(8,128)(2,1)S(1)}, u32[]{:S(2)}, u32[]{:S(2)}) collective-permute-start(bf16[6,128,512]{1,2,0:T(8,128)(2,1)} %collective-permute-done.1), channel_id=1, source_target_pairs={{0,28},{4,0},{8,4},{12,8},{16,12},{20,16},{24,20},{28,24},{1,29},{... | collective-permute-start | bytes 2359304 | tf_op jit(solution)/shard_map/ppermute | solution.py:25
  63.1 33.5 %collective-permute-done.2 = bf16[6,128,512]{1,2,0:T(8,128)(2,1)S(1)} collective-permute-done((bf16[6,128,512]{1,2,0:T(8,128)(2,1)}, bf16[6,128,512]{1,2,0:T(8,128)(2,1)S(1)}, u32[]{:S(2)}, u32[]{:S(2)}) %collective-permute-start.2) | collective-permute-done | bytes 786464 | tf_op jit(solution)/shard_map/ppermute | solution.py:20
  96.5 2.4 collective-permute-start.4
  99.6 1.7 fusion
  101.3 0.9 fusion.1
  102.7 3.1 %collective-permute-start.5 = (bf16[6,128,512]{1,2,0:T(8,128)(2,1)S(1)}, bf16[6,128,512]{1,2,0:T(8,128)(2,1)S(1)}, u32[]{:S(2)}, u32[]{:S(2)}) collective-permute-start(bf16[6,128,512]{1,2,0:T(8,128)(2,1)S(1)} %collective-permute-done.3), channel_id=1, source_target_pairs={{0,28},{4,0},{8,4},{12,8},{16,12},{20,16},{24,20},{28,24},{1,29},{... | collective-permute-start | bytes 2359304 | tf_op jit(solution)/shard_map/ppermute | solution.py:25
  106.9 41.7 %collective-permute-done.4 = bf16[6,128,512]{1,2,0:T(8,128)(2,1)S(1)} collective-permute-done((bf16[6,128,512]{1,2,0:T(8,128)(2,1)S(1)}, bf16[6,128,512]{1,2,0:T(8,128)(2,1)S(1)}, u32[]{:S(2)}, u32[]{:S(2)}) %collective-permute-start.4) | collective-permute-done | bytes 786464 | tf_op jit(solution)/shard_map/ppermute | solution.py:20
  148.6 2.5 %collective-permute-start.6 = (bf16[6,128,512]{1,2,0:T(8,128)(2,1)S(1)}, bf16[6,128,512]{1,2,0:T(8,128)(2,1)S(1)}, u32[]{:S(2)}, u32[]{:S(2)}) collective-permute-start(bf16[6,128,512]{1,2,0:T(8,128)(2,1)S(1)} %collective-permute-done.4), channel_id=1, source_target_pairs={{0,4},{4,8},{8,12},{12,16},{16,20},{20,24},{24,28},{28,0},{1,5},{5... | collective-permute-start | bytes 2359304 | tf_op jit(solution)/shard_map/ppermute | solution.py:20
  151.1 1.4 constant_dynamic-update-slice_fusion.6
  152.5 1.4 constant_dynamic-update-slice_fusion.5
  154.8 13.4 %collective-permute-done.5 = bf16[6,128,512]{1,2,0:T(8,128)(2,1)S(1)} collective-permute-done((bf16[6,128,512]{1,2,0:T(8,128)(2,1)S(1)}, bf16[6,128,512]{1,2,0:T(8,128)(2,1)S(1)}, u32[]{:S(2)}, u32[]{:S(2)}) %collective-permute-start.5) | collective-permute-done | bytes 786464 | tf_op jit(solution)/shard_map/ppermute | solution.py:25
  168.5 7.0 %collective-permute-done.6 = bf16[6,128,512]{1,2,0:T(8,128)(2,1)S(1)} collective-permute-done((bf16[6,128,512]{1,2,0:T(8,128)(2,1)S(1)}, bf16[6,128,512]{1,2,0:T(8,128)(2,1)S(1)}, u32[]{:S(2)}, u32[]{:S(2)}) %collective-permute-start.6) | collective-permute-done | bytes 786464 | tf_op jit(solution)/shard_map/ppermute | solution.py:20
  180.1 1.2 copy-done.7
  181.8 17.3 %all-gather.2.cloned.1.call-done = bf16[6,1024,512]{1,2,0:T(8,128)(2,1)} async-done(((bf16[6,128,512]{1,2,0:T(8,128)(2,1)}), bf16[6,1024,512]{1,2,0:T(8,128)(2,1)}) %all-gather.2.cloned.1.call-update) | async-done | bytes 6291472 | tf_op jit(solution)/shard_map/all_gather | solution.py:132
  199.1 1.8 constant_dynamic-slice_fusion.4
  203.4 1.0 fusion.31
  206.8 1.5 convolution_convert_fusion
  208.3 22.2 %reduce-scatter.2.cloned.1.call-done = bf16[192,512]{1,0:T(8,128)(2,1)} async-done(((bf16[192,2048]{1,0:T(8,128)(2,1)}), bf16[192,512]{1,0:T(8,128)(2,1)}) %reduce-scatter.2.cloned.1.call-update) | async-done | bytes 196624 | tf_op jit(solution)/shard_map/reduce_scatter | solution.py:148
  230.5 1.7 add_convert_fusion
  (78 shorter events, 18.0 us)
Async XLA Ops:
  6.5 200.2 %copy-start = (bf16[512,2048]{1,0:T(8,128)(2,1)S(1)}, bf16[512,2048]{1,0:T(8,128)(2,1)}, u32[]{:S(2)}) copy-start(bf16[512,2048]{1,0:T(8,128)(2,1)} %param.18) | copy-start | bytes 6291460
  6.5 192.5 %all-gather.2.cloned.1.call-start = ((), (), s32[]{:S(2)}) async-start(), calls=%async_computation.1 | async-start | bytes 7077888 | tf_op jit(solution)/shard_map/all_gather | solution.py:132
  9.0 7.7 %copy-start.15 = (s32[8]{0:T(128)S(1)}, s32[8]{0:T(128)}, u32[]{:S(2)}) copy-start(s32[8]{0:T(128)} %param.24) | copy-start | bytes 100
  9.0 7.7 %copy-start.16 = (s32[8]{0:T(128)S(1)}, s32[8]{0:T(128)}, u32[]{:S(2)}) copy-start(s32[8]{0:T(128)} %param.27) | copy-start | bytes 100
  9.0 9.7 %copy-start.18 = (s32[4]{0:T(128)S(1)}, s32[4]{0:T(128)}, u32[]{:S(2)}) copy-start(s32[4]{0:T(128)} %param.25) | copy-start | bytes 52
  9.0 221.5 %reduce-scatter.2.cloned.1.call-start = ((), (), s32[]{:S(2)}) async-start(), calls=%async_computation.2 | async-start | bytes 983040 | tf_op jit(solution)/shard_map/reduce_scatter | solution.py:148
  10.6 45.1 %collective-permute-start = (bf16[6,128,512]{1,2,0:T(8,128)(2,1)S(1)}, bf16[6,128,512]{1,2,0:T(8,128)(2,1)}, u32[]{:S(2)}, u32[]{:S(2)}) collective-permute-start(bf16[6,128,512]{1,2,0:T(8,128)(2,1)S(1)} %copy.27), channel_id=1, source_target_pairs={{0,4},{4,8},{8,12},{12,16},{16,20},{20,24},{24,28},{28,0},{1,5},{5... | collective-permute-start | bytes 2359304 | tf_op jit(solution)/shard_map/ppermute | solution.py:20
  13.6 45.7 %collective-permute-start.1 = (bf16[6,128,512]{1,2,0:T(8,128)(2,1)S(1)}, bf16[6,128,512]{1,2,0:T(8,128)(2,1)}, u32[]{:S(2)}, u32[]{:S(2)}) collective-permute-start(bf16[6,128,512]{1,2,0:T(8,128)(2,1)S(1)} %copy.27), channel_id=1, source_target_pairs={{0,28},{4,0},{8,4},{12,8},{16,12},{20,16},{24,20},{28,24},{1,29},{... | collective-permute-start | bytes 2359304 | tf_op jit(solution)/shard_map/ppermute | solution.py:25
  22.7 6.5 %copy-start.17 = (s32[6]{0:T(128)S(1)}, s32[6]{0:T(128)}, u32[]{:S(2)}) copy-start(s32[6]{0:T(128)} %param.26) | copy-start | bytes 76
  22.7 8.6 %copy-start.19 = (s32[8]{0:T(128)S(1)}, s32[8]{0:T(128)}, u32[]{:S(2)}) copy-start(s32[8]{0:T(128)} %param.23) | copy-start | bytes 100
  23.8 34.5 %copy-start.13 = (bf16[192,512]{1,0:T(8,128)(2,1)S(1)}, bf16[192,512]{1,0:T(8,128)(2,1)}, u32[]{:S(2)}) copy-start(bf16[192,512]{1,0:T(8,128)(2,1)} %param.15) | copy-start | bytes 589828
  23.8 75.8 %copy-start.9 = (bf16[192,512]{1,0:T(8,128)(2,1)S(1)}, bf16[192,512]{1,0:T(8,128)(2,1)}, u32[]{:S(2)}) copy-start(bf16[192,512]{1,0:T(8,128)(2,1)} %param.14) | copy-start | bytes 589828
  55.7 40.9 %collective-permute-start.2 = (bf16[6,128,512]{1,2,0:T(8,128)(2,1)}, bf16[6,128,512]{1,2,0:T(8,128)(2,1)S(1)}, u32[]{:S(2)}, u32[]{:S(2)}) collective-permute-start(bf16[6,128,512]{1,2,0:T(8,128)(2,1)} %collective-permute-done), channel_id=1, source_target_pairs={{0,4},{4,8},{8,12},{12,16},{16,20},{20,24},{24,28},{28,0},{1,5},{5... | collective-permute-start | bytes 2359304 | tf_op jit(solution)/shard_map/ppermute | solution.py:20
  59.3 43.2 %collective-permute-start.3 = (bf16[6,128,512]{1,2,0:T(8,128)(2,1)}, bf16[6,128,512]{1,2,0:T(8,128)(2,1)S(1)}, u32[]{:S(2)}, u32[]{:S(2)}) collective-permute-start(bf16[6,128,512]{1,2,0:T(8,128)(2,1)} %collective-permute-done.1), channel_id=1, source_target_pairs={{0,28},{4,0},{8,4},{12,8},{16,12},{20,16},{24,20},{28,24},{1,29},{... | collective-permute-start | bytes 2359304 | tf_op jit(solution)/shard_map/ppermute | solution.py:25
  96.5 52.1 %collective-permute-start.4 = (bf16[6,128,512]{1,2,0:T(8,128)(2,1)S(1)}, bf16[6,128,512]{1,2,0:T(8,128)(2,1)S(1)}, u32[]{:S(2)}, u32[]{:S(2)}) collective-permute-start(bf16[6,128,512]{1,2,0:T(8,128)(2,1)S(1)} %collective-permute-done.2), channel_id=1, source_target_pairs={{0,4},{4,8},{8,12},{12,16},{16,20},{20,24},{24,28},{28,0},{1,5},{5... | collective-permute-start | bytes 2359304 | tf_op jit(solution)/shard_map/ppermute | solution.py:20
  101.3 1.4 copy-start.10
  102.7 65.4 %collective-permute-start.5 = (bf16[6,128,512]{1,2,0:T(8,128)(2,1)S(1)}, bf16[6,128,512]{1,2,0:T(8,128)(2,1)S(1)}, u32[]{:S(2)}, u32[]{:S(2)}) collective-permute-start(bf16[6,128,512]{1,2,0:T(8,128)(2,1)S(1)} %collective-permute-done.3), channel_id=1, source_target_pairs={{0,28},{4,0},{8,4},{12,8},{16,12},{20,16},{24,20},{28,24},{1,29},{... | collective-permute-start | bytes 2359304 | tf_op jit(solution)/shard_map/ppermute | solution.py:25
  148.6 26.8 %collective-permute-start.6 = (bf16[6,128,512]{1,2,0:T(8,128)(2,1)S(1)}, bf16[6,128,512]{1,2,0:T(8,128)(2,1)S(1)}, u32[]{:S(2)}, u32[]{:S(2)}) collective-permute-start(bf16[6,128,512]{1,2,0:T(8,128)(2,1)S(1)} %collective-permute-done.4), channel_id=1, source_target_pairs={{0,4},{4,8},{8,12},{12,16},{16,20},{20,24},{24,28},{28,0},{1,5},{5... | collective-permute-start | bytes 2359304 | tf_op jit(solution)/shard_map/ppermute | solution.py:20
  176.5 1.2 copy-start.3
  177.7 1.2 copy-start.5
  178.9 1.2 copy-start.1
  180.1 1.2 copy-start.7
  199.1 2.0 copy-start.6
  200.8 1.5 copy-start.8
  201.1 1.7 copy-start.12
  201.6 1.8 copy-start.11
  203.4 1.4 copy-start.2
  204.8 1.4 copy-start.4
  206.7 23.8 %copy-start.14 = (bf16[192,512]{1,0:T(8,128)(2,1)S(1)}, bf16[192,512]{1,0:T(8,128)(2,1)}, u32[]{:S(2)}) copy-start(bf16[192,512]{1,0:T(8,128)(2,1)} %param.17) | copy-start | bytes 589828
Sparse Core Ops, SparseCore 0:
  9.4 189.6 all-gather.1
  208.4 22.0 reduce-scatter.1
